TPU v7x, 32 devices: a whole 2x2x4 slice. The times are simulated.
32 devices in a mesh: node: 8 (over z, x), feat: 4 (over y, core).
Axes of the slice: x: 2, y: 2, z: 4, core: 2. Of those that a mesh axis runs over, the one named last changes fastest.
Arguments:
- features: bfloat16 [128, 128, 128], P('node', 'feat'), may hold values from -6 to 6
- tile_values: bfloat16 [2048, 128, 128], P('node'), may hold values from -0.125 to 0.125
- tile_row: int32 [2048], P('node'), may hold values from 0 to 127, as said below
- tile_col: int32 [2048], P('node'), may hold values from 0 to 127, as said below
- tile_count: int32 [8], P('node'), may hold values from 32 to 256, as said below
- weight: float32 [128, 128], P('feat'), may hold values from -0.5 to 0.5
- first_moment: float32 [128, 128], P('feat'), may hold values from -3 to 3
- second_moment: float32 [128, 128], P('feat'), may hold values from 0.1 to 2
- cotangent: bfloat16 [128, 128, 128], P('node', 'feat'), may hold values from -6 to 6
Outputs:
- activated: bfloat16 [128, 128, 128], P('node', 'feat')
- feature_grad: float32 [128, 128, 128], P('node', 'feat')
- new_weight: float32 [128, 128], P('feat')
- new_first: float32 [128, 128], P('feat')
- new_second: float32 [128, 128], P('feat')
Inputs may be any that keep to these rules, and one draw needn't show every extreme that they name: `tile_row`: the slots of index d of node (slots d * 256 to (d + 1) * 256 - 1) name target blocks of that index only: d * 16 to (d + 1) * 16 - 1. `tile_col`: A slot's source block lies on an index of node at most 2 away from the slot's own index around the closed loop of node indices; both distances 2 occur on every index. `tile_count`: some index of node has all 256 slots live, some has 32.
All inputs are finite; a program needn't handle non-finite values.
Results may differ from a plain program's by a relative error of at most 0.0058.
Values may be sent and summed in bfloat16 or wider, within the bound.
No kernel may reach another device: no remote copies, remote signals or barrier semaphores. Data moves between devices by JAX's collectives and lax.ppermute only.
A program may use at most 64 MiB of HBM per device.

v0:
```python
import math
import jax
import jax.numpy as jnp
from jax import lax
from jax.sharding import PartitionSpec as P

REACH = 2
first_decay = 0.9
second_decay = 0.999
learn_rate = 0.05
first_fix = 1.0 - 0.9**10
second_fix = 1.0 - 0.999**10
adam_eps = 1e-08


def passed_along(block, axis, distance):
    devices = range(lax.axis_size(axis))
    route = [((i - distance) % len(devices), i) for i in devices]
    return lax.ppermute(block, axis, route)


def elu_slope(preact):
    return jnp.where(preact > 0, 1.0, jnp.exp(jnp.minimum(preact, 0.0)))


def one_hot_table(indices, count, dtype):
    return (indices[:, None] == jnp.arange(count)[None, :]).astype(dtype)


def per_device(
    features,
    tile_values,
    tile_row,
    tile_col,
    tile_count,
    weight,
    first_moment,
    second_moment,
    cotangent,
):
    cycle_size = lax.axis_size("node")
    own_node = lax.axis_index("node")
    blocks = features.shape[0]
    width_local = features.shape[1]
    tile_size = features.shape[2]
    slots = tile_values.shape[0]
    live = (jnp.arange(slots) < tile_count[0]).astype(jnp.float32)
    local_row = tile_row - own_node * blocks
    col_owner = tile_col // blocks
    col_block = tile_col % blocks
    offset = (col_owner - own_node) % cycle_size
    offset = jnp.where(offset > cycle_size // 2, offset - cycle_size, offset)
    source_slot = (offset + REACH) * blocks + col_block
    targets = (2 * REACH + 1) * blocks
    pick_source = one_hot_table(source_slot, targets, jnp.bfloat16)
    pick_row = one_hot_table(local_row, blocks, jnp.bfloat16)
    add_row = one_hot_table(local_row, blocks, jnp.float32) * live[:, None]
    add_source = one_hot_table(source_slot, targets, jnp.float32) * live[:, None]
    pieces = []
    for distance in range(-REACH, REACH + 1):
        if distance == 0:
            pieces.append(features)
        else:
            pieces.append(passed_along(features, "node", -distance))
    nearby = jnp.concatenate(pieces, axis=0)
    sources = jnp.einsum(
        "ts,sfk->tfk", pick_source, nearby, preferred_element_type=jnp.float32
    ).astype(jnp.bfloat16)
    forward_terms = jnp.einsum(
        "tfk,tjk->tfj", sources, tile_values, preferred_element_type=jnp.float32
    )
    aggregate = jnp.einsum("tb,tfj->bfj", add_row, forward_terms, precision=lax.Precision.HIGHEST)
    aggregate = aggregate.astype(jnp.bfloat16)
    weight_half = weight.astype(jnp.bfloat16)
    aggregate_all, weight_all = (
        lax.all_gather(aggregate, "feat", axis=1, tiled=True),
        lax.all_gather(weight_half, "feat", axis=0, tiled=True),
    )
    column_start = lax.axis_index("feat") * width_local
    weight_cols = lax.dynamic_slice_in_dim(weight_all, column_start, width_local, 1)
    preact = jnp.einsum(
        "bij,io->boj", aggregate_all, weight_cols, preferred_element_type=jnp.float32
    )
    activated = jax.nn.elu(preact).astype(jnp.bfloat16)
    slope_grad = (cotangent.astype(jnp.float32) * elu_slope(preact)).astype(jnp.bfloat16)
    slope_all = lax.all_gather(slope_grad, "feat", axis=1, tiled=True)
    node_total = cycle_size * blocks * tile_size
    grad_local = jnp.einsum("bij,boj->io", aggregate, slope_all, preferred_element_type=jnp.float32)
    grad = lax.psum(grad_local, "node") * (1.0 / math.sqrt(node_total))
    back_rows = jnp.einsum(
        "io,boj->bij", weight_half, slope_all, preferred_element_type=jnp.float32
    ).astype(jnp.bfloat16)
    back_sources = jnp.einsum(
        "tb,bfj->tfj", pick_row, back_rows, preferred_element_type=jnp.float32
    ).astype(jnp.bfloat16)
    back_terms = jnp.einsum(
        "tfj,tjk->tfk", back_sources, tile_values, preferred_element_type=jnp.float32
    )
    outgoing = jnp.einsum("ts,tfk->sfk", add_source, back_terms, precision=lax.Precision.HIGHEST)
    outgoing = outgoing.reshape(2 * REACH + 1, blocks, width_local, tile_size)
    feature_grad = outgoing[REACH]
    for distance in range(-REACH, REACH + 1):
        if distance != 0:
            feature_grad = feature_grad + passed_along(outgoing[distance + REACH], "node", distance)
    new_first = first_decay * first_moment + (1.0 - first_decay) * grad
    new_second = second_decay * second_moment + (1.0 - second_decay) * grad * grad
    new_weight = weight - learn_rate * (new_first / first_fix) / (
        jnp.sqrt(new_second / second_fix) + adam_eps
    )
    return (activated, feature_grad, new_weight, new_first, new_second)


def solution(mesh):
    return jax.shard_map(
        per_device,
        mesh=mesh,
        in_specs=(
            P("node", "feat", None),
            P("node", None, None),
            P("node"),
            P("node"),
            P("node"),
            P("feat", None),
            P("feat", None),
            P("feat", None),
            P("node", "feat", None),
        ),
        out_specs=(
            P("node", "feat", None),
            P("node", "feat", None),
            P("feat", None),
            P("feat", None),
            P("feat", None),
        ),
        check_vma=False,
    )
```

profile of v0, /device:TPU:0, one launch (start us, length us, event | category | flops | bytes accessed | tf_op | source)
XLA Modules:
  0.0 112.7 jit_solution(17020929460422994571)
XLA Ops:
  0.6 6.0 %collective-permute-start.2 = (bf16[16,32,128]{2,1,0:T(8,128)(2,1)}, bf16[16,32,128]{2,1,0:T(8,128)(2,1)S(1)}, u32[]{:S(2)}, u32[]{:S(2)}) collective-permute-start(bf16[16,32,128]{2,1,0:T(8,128)(2,1)} %param.9), channel_id=1, source_target_pairs={{4,0},{8,4},{12,8},{16,12},{20,16},{24,20},{28,24},{0,28},{5,1},{9... | collective-permute-start | bytes 393224 | tf_op jit(solution)/shard_map/ppermute | solution.py:19
  6.7 3.8 %collective-permute-start.3 = (bf16[16,32,128]{2,1,0:T(8,128)(2,1)}, bf16[16,32,128]{2,1,0:T(8,128)(2,1)S(1)}, u32[]{:S(2)}, u32[]{:S(2)}) collective-permute-start(bf16[16,32,128]{2,1,0:T(8,128)(2,1)} %param.9), channel_id=1, source_target_pairs={{8,0},{12,4},{16,8},{20,12},{24,16},{28,20},{0,24},{4,28},{9,1},{1... | collective-permute-start | bytes 393224 | tf_op jit(solution)/shard_map/ppermute | solution.py:19
  10.5 0.7 fusion.41
  11.2 0.7 broadcast_subtract_fusion
  12.5 0.7 convert_element_type.38
  13.3 5.2 %all_gather.9 = bf16[128,128]{1,0:T(8,128)(2,1)S(1)} all-gather(bf16[32,128]{1,0:T(8,128)(2,1)S(1)} %convert_element_type.38), channel_id=1, replica_groups=mesh['node'=8,'feat'=4] {'feat'}, dimensions={0}, use_global_device_ids=true | all-gather | bytes 40960 | tf_op jit(solution)/shard_map/all_gather | solution.py:77
  18.5 0.9 constant_dynamic-update-slice_fusion.2
  19.5 0.8 fusion.10
  20.3 7.2 %fusion.4 = f32[256,32,128]{2,1,0:T(8,128)S(1)} fusion(bf16[256,128,128]{2,1,0:T(8,128)(2,1)} %param.10, bf16[256,32,128]{2,0,1:T(8,128)(2,1)S(1)} %fusion.10), kind=kOutput, calls=%fused_computation.6 | convolution fusion | flops 268435456 | bytes 14680064 | tf_op jit(solution)/shard_map/tfk,tjk->tfj/dot_general | solution.py:69
  27.5 4.4 %fusion.7 = bf16[16,32,128]{2,0,1:T(8,128)(2,1)S(1)} fusion(f32[256,32,128]{2,1,0:T(8,128)S(1)} %fusion.4, f32[256]{0:T(256)S(1)} %compare_convert_fusion, s32[256]{0:T(256)S(1)} %broadcast_subtract_fusion), kind=kOutput, calls=%fused_computation.11 | convolution fusion | flops 201400320 | bytes 4327424 | tf_op jit(solution)/shard_map/tb,tfj->bfj/dot_general | solution.py:72
  31.9 7.3 %all_gather.10 = bf16[16,128,128]{2,0,1:T(8,128)(2,1)S(1)} all-gather(bf16[16,32,128]{2,0,1:T(8,128)(2,1)S(1)} %fusion.7), channel_id=1, replica_groups=mesh['node'=8,'feat'=4] {'feat'}, dimensions={1}, use_global_device_ids=true | all-gather | bytes 655360 | tf_op jit(solution)/shard_map/all_gather | solution.py:76
  39.1 1.1 fusion.16
  40.2 7.5 %all_gather.11 = bf16[16,128,128]{2,1,0:T(8,128)(2,1)S(1)} all-gather(bf16[16,32,128]{2,1,0:T(8,128)(2,1)S(1)} %get-tuple-element.22), channel_id=1, replica_groups=mesh['node'=8,'feat'=4] {'feat'}, dimensions={1}, use_global_device_ids=true | all-gather | bytes 655360 | tf_op jit(solution)/shard_map/all_gather | solution.py:86
  48.3 0.7 fusion.34
  49.0 7.2 %fusion.5 = f32[256,32,128]{2,1,0:T(8,128)S(1)} fusion(bf16[256,128,128]{2,1,0:T(8,128)(2,1)} %param.10, bf16[256,32,128]{2,0,1:T(8,128)(2,1)S(1)} %fusion.34), kind=kOutput, calls=%fused_computation.7 | convolution fusion | flops 268435456 | bytes 14680064 | tf_op jit(solution)/shard_map/tfj,tjk->tfk/dot_general | solution.py:96
  56.2 4.9 %fusion = f32[80,32,128]{2,0,1:T(8,128)S(1)} fusion(f32[256,32,128]{2,1,0:T(8,128)S(1)} %fusion.5, f32[256]{0:T(256)S(1)} %compare_convert_fusion, s32[256]{0:T(256)S(1)} %fusion.41), kind=kOutput, calls=%fused_computation | convolution fusion | flops 1006673920 | bytes 5507072 | tf_op jit(solution)/shard_map/ts,tfk->sfk/dot_general | solution.py:99
  61.1 0.9 fusion.48
  62.0 2.0 %collective-permute-start.7 = (f32[16,32,128]{2,0,1:T(8,128)}, f32[16,32,128]{2,0,1:T(8,128)S(1)}, u32[]{:S(2)}, u32[]{:S(2)}) collective-permute-start(f32[16,32,128]{2,0,1:T(8,128)} %get-tuple-element.19), channel_id=1, source_target_pairs={{24,0},{28,4},{0,8},{4,12},{8,16},{12,20},{16,24},{20,28},{25,1},{... | collective-permute-start | bytes 786440 | tf_op jit(solution)/shard_map/ppermute | solution.py:19
  64.0 1.5 %collective-permute-start.6 = (f32[16,32,128]{2,0,1:T(8,128)S(1)}, f32[16,32,128]{2,0,1:T(8,128)S(1)}, u32[]{:S(2)}, u32[]{:S(2)}) collective-permute-start(f32[16,32,128]{2,0,1:T(8,128)S(1)} %get-tuple-element.20), channel_id=1, source_target_pairs={{28,0},{0,4},{4,8},{8,12},{12,16},{16,20},{20,24},{24,28},{29,1},{... | collective-permute-start | bytes 786440 | tf_op jit(solution)/shard_map/ppermute | solution.py:19
  65.5 3.3 %collective-permute-start.5 = (f32[16,32,128]{2,0,1:T(8,128)S(1)}, f32[16,32,128]{2,0,1:T(8,128)S(1)}, u32[]{:S(2)}, u32[]{:S(2)}) collective-permute-start(f32[16,32,128]{2,0,1:T(8,128)S(1)} %get-tuple-element.21), channel_id=1, source_target_pairs={{4,0},{8,4},{12,8},{16,12},{20,16},{24,20},{28,24},{0,28},{5,1},{9... | collective-permute-start | bytes 786440 | tf_op jit(solution)/shard_map/ppermute | solution.py:19
  68.8 0.9 convolution_bitcast_fusion.1
  69.7 40.8 %psum.7 = f32[32,128]{1,0:T(8,128)S(1)} all-reduce(f32[32,128]{1,0:T(8,128)} %convolution_bitcast_fusion.1), channel_id=1, replica_groups=mesh['node'=8,'feat'=4] {'node'}, use_global_device_ids=true, to_apply=%region_0.1 | all-reduce | flops 4096 | bytes 32768 | tf_op jit(solution)/shard_map/psum | solution.py:89
  110.4 1.4 %divide_subtract_fusion = (f32[32,128]{1,0:T(8,128)}, f32[32,128]{1,0:T(8,128)}, f32[32,128]{1,0:T(8,128)}) fusion(f32[32,128]{1,0:T(8,128)S(1)} %copy-done, f32[32,128]{1,0:T(8,128)S(1)} %psum.7, f32[32,128]{1,0:T(8,128)} %param.15, f32[32,128]{1,0:T(8,128)} %param.16), kind=kLoop, calls=%fused_computation.39 | loop fusion | flops 53248 | bytes 114688 | tf_op jit(solution)/shard_map/sub | solution.py:107
  111.9 0.8 copy.21
  (23 shorter events, 0.8 us)
Async XLA Ops:
  0.6 18.8 %collective-permute-start.2 = (bf16[16,32,128]{2,1,0:T(8,128)(2,1)}, bf16[16,32,128]{2,1,0:T(8,128)(2,1)S(1)}, u32[]{:S(2)}, u32[]{:S(2)}) collective-permute-start(bf16[16,32,128]{2,1,0:T(8,128)(2,1)} %param.9), channel_id=1, source_target_pairs={{4,0},{8,4},{12,8},{16,12},{20,16},{24,20},{28,24},{0,28},{5,1},{9... | collective-permute-start | bytes 393224 | tf_op jit(solution)/shard_map/ppermute | solution.py:19
  6.7 11.8 %collective-permute-start.1 = (bf16[16,32,128]{2,1,0:T(8,128)(2,1)}, bf16[16,32,128]{2,1,0:T(8,128)(2,1)S(1)}, u32[]{:S(2)}, u32[]{:S(2)}) collective-permute-start(bf16[16,32,128]{2,1,0:T(8,128)(2,1)} %param.9), channel_id=1, source_target_pairs={{28,0},{0,4},{4,8},{8,12},{12,16},{16,20},{20,24},{24,28},{29,1},{... | collective-permute-start | bytes 393224 | tf_op jit(solution)/shard_map/ppermute | solution.py:19
  6.7 11.8 %collective-permute-start = (bf16[16,32,128]{2,1,0:T(8,128)(2,1)}, bf16[16,32,128]{2,1,0:T(8,128)(2,1)S(1)}, u32[]{:S(2)}, u32[]{:S(2)}) collective-permute-start(bf16[16,32,128]{2,1,0:T(8,128)(2,1)} %param.9), channel_id=1, source_target_pairs={{24,0},{28,4},{0,8},{4,12},{8,16},{12,20},{16,24},{20,28},{25,1},{... | collective-permute-start | bytes 393224 | tf_op jit(solution)/shard_map/ppermute | solution.py:19
  6.7 12.8 %collective-permute-start.3 = (bf16[16,32,128]{2,1,0:T(8,128)(2,1)}, bf16[16,32,128]{2,1,0:T(8,128)(2,1)S(1)}, u32[]{:S(2)}, u32[]{:S(2)}) collective-permute-start(bf16[16,32,128]{2,1,0:T(8,128)(2,1)} %param.9), channel_id=1, source_target_pairs={{8,0},{12,4},{16,8},{20,12},{24,16},{28,20},{0,24},{4,28},{9,1},{1... | collective-permute-start | bytes 393224 | tf_op jit(solution)/shard_map/ppermute | solution.py:19
  27.5 11.6 %copy-start.1 = (bf16[16,32,128]{2,1,0:T(8,128)(2,1)S(1)}, bf16[16,32,128]{2,1,0:T(8,128)(2,1)}, u32[]{:S(2)}) copy-start(bf16[16,32,128]{2,1,0:T(8,128)(2,1)} %param.17) | copy-start | bytes 393220
  56.2 54.2 %copy-start = (f32[32,128]{1,0:T(8,128)S(1)}, f32[32,128]{1,0:T(8,128)}, u32[]{:S(2)}) copy-start(f32[32,128]{1,0:T(8,128)} %param.14) | copy-start | bytes 49156
  62.0 49.8 %collective-permute-start.4 = (f32[16,32,128]{2,0,1:T(8,128)}, f32[16,32,128]{2,0,1:T(8,128)S(1)}, u32[]{:S(2)}, u32[]{:S(2)}) collective-permute-start(f32[16,32,128]{2,0,1:T(8,128)} %get-tuple-element.18), channel_id=1, source_target_pairs={{8,0},{12,4},{16,8},{20,12},{24,16},{28,20},{0,24},{4,28},{9,1},{1... | collective-permute-start | bytes 786440 | tf_op jit(solution)/shard_map/ppermute | solution.py:19
  62.0 49.8 %collective-permute-start.7 = (f32[16,32,128]{2,0,1:T(8,128)}, f32[16,32,128]{2,0,1:T(8,128)S(1)}, u32[]{:S(2)}, u32[]{:S(2)}) collective-permute-start(f32[16,32,128]{2,0,1:T(8,128)} %get-tuple-element.19), channel_id=1, source_target_pairs={{24,0},{28,4},{0,8},{4,12},{8,16},{12,20},{16,24},{20,28},{25,1},{... | collective-permute-start | bytes 786440 | tf_op jit(solution)/shard_map/ppermute | solution.py:19
  64.0 47.7 %collective-permute-start.6 = (f32[16,32,128]{2,0,1:T(8,128)S(1)}, f32[16,32,128]{2,0,1:T(8,128)S(1)}, u32[]{:S(2)}, u32[]{:S(2)}) collective-permute-start(f32[16,32,128]{2,0,1:T(8,128)S(1)} %get-tuple-element.20), channel_id=1, source_target_pairs={{28,0},{0,4},{4,8},{8,12},{12,16},{16,20},{20,24},{24,28},{29,1},{... | collective-permute-start | bytes 786440 | tf_op jit(solution)/shard_map/ppermute | solution.py:19
  65.5 46.3 %collective-permute-start.5 = (f32[16,32,128]{2,0,1:T(8,128)S(1)}, f32[16,32,128]{2,0,1:T(8,128)S(1)}, u32[]{:S(2)}, u32[]{:S(2)}) collective-permute-start(f32[16,32,128]{2,0,1:T(8,128)S(1)} %get-tuple-element.21), channel_id=1, source_target_pairs={{4,0},{8,4},{12,8},{16,12},{20,16},{24,20},{28,24},{0,28},{5,1},{9... | collective-permute-start | bytes 786440 | tf_op jit(solution)/shard_map/ppermute | solution.py:19
where the time goes:
time: 113 us
  blocking collectives  60.6 us (54%)
  matrix products  27.5 us (24%)
  starting transfers between devices  16.6 us (15%)
  other arithmetic  3.56 us (3%)
  local copies, waits for them, and re-layouts  2.92 us (3%)
  between operations  1.42 us (1%)
    psum x1, blocking collectives, per_device(): grad = lax.psum(grad_local, 'node') * (1.0 / math.sqrt(node_total))  40.8 us
    ppermute x8, starting transfers between devices, passed_along(): return lax.ppermute(block, axis, route)  16.6 us
    all_gather x1, blocking collectives, per_device(): slope_all = lax.all_gather(slope_grad, 'feat', axis=1, tiled=True)  7.46 us
    all_gather x1, blocking collectives, per_device(): lax.all_gather(aggregate, 'feat', axis=1, tiled=True)  7.25 us
    dot_general x1, matrix products, per_device(): jnp.einsum('tfk,tjk->tfj', sources, tile_values, preferred_element_type=j...  7.25 us
    dot_general x1, matrix products, per_device(): jnp.einsum('tfj,tjk->tfk', back_sources, tile_values, preferred_element_t...  7.21 us
    all_gather x1, blocking collectives, per_device(): lax.all_gather(weight_half, 'feat', axis=0, tiled=True)  5.18 us
    dot_general x1, matrix products, per_device(): jnp.einsum('ts,tfk->sfk', add_source, back_terms, precision=lax.Precision...  4.89 us
  transfers between devices with their start and end apart: 8, of which 0 were waited for; matrix products, arithmetic and copies ran while one was open for 5% of the time, Pallas kernels for 0%

commit v1 on v0

--- a/solution.py
+++ b/solution.py
@@ -86,7 +86,7 @@
     slope_all = lax.all_gather(slope_grad, "feat", axis=1, tiled=True)
     node_total = cycle_size * blocks * tile_size
     grad_local = jnp.einsum("bij,boj->io", aggregate, slope_all, preferred_element_type=jnp.float32)
-    grad = lax.psum(grad_local, "node") * (1.0 / math.sqrt(node_total))
+    grad = jnp.sum(lax.all_gather(grad_local, "node"), axis=0) * (1.0 / math.sqrt(node_total))
     back_rows = jnp.einsum(
         "io,boj->bij", weight_half, slope_all, preferred_element_type=jnp.float32
     ).astype(jnp.bfloat16)

time: 113 us -> 109 us (0.965)
  blocking collectives: 60.6 us -> 57.8 us
    psum x1 -> x0, blocking collectives: 40.8 us -> none  [per_device(): grad = lax.psum(grad_local, 'node') * (1.0 / math.sqrt(node_total))]
    all_gather x0 -> x1, blocking collectives: none -> 37.9 us  [per_device(): lax.all_gather(grad_local, 'node')]
  transfers between devices with their start and end apart: 8 -> 8, of which waited for: 0 -> 0; matrix products, arithmetic and copies ran while one was open for 5% -> 4% of each run, Pallas kernels for 0% -> 0%
where the time goes in v1:
time: 109 us
  blocking collectives  57.8 us (53%)
  matrix products  26.9 us (25%)
  starting transfers between devices  16.6 us (15%)
  other arithmetic  3.59 us (3%)
  local copies, waits for them, and re-layouts  2.1 us (2%)
  between operations  1.44 us (1%)
    all_gather x1, blocking collectives, per_device(): lax.all_gather(grad_local, 'node')  37.9 us
    ppermute x8, starting transfers between devices, passed_along(): return lax.ppermute(block, axis, route)  16.6 us
    all_gather x1, blocking collectives, per_device(): slope_all = lax.all_gather(slope_grad, 'feat', axis=1, tiled=True)  7.46 us
    all_gather x1, blocking collectives, per_device(): lax.all_gather(aggregate, 'feat', axis=1, tiled=True)  7.25 us
    dot_general x1, matrix products, per_device(): jnp.einsum('tfk,tjk->tfj', sources, tile_values, preferred_element_type=j...  7.25 us
    dot_general x1, matrix products, per_device(): jnp.einsum('tfj,tjk->tfk', back_sources, tile_values, preferred_element_t...  7.21 us
    all_gather x1, blocking collectives, per_device(): lax.all_gather(weight_half, 'feat', axis=0, tiled=True)  5.18 us
    dot_general x1, matrix products, per_device(): jnp.einsum('ts,tfk->sfk', add_source, back_terms, precision=lax.Precision...  4.89 us
  transfers between devices with their start and end apart: 8, of which 0 were waited for; matrix products, arithmetic and copies ran while one was open for 4% of the time, Pallas kernels for 0%

profile of v1, /device:TPU:0, one launch (start us, length us, event | category | flops | bytes accessed | tf_op | source)
XLA Modules:
  0.0 108.5 jit_solution(9557402522557386790)
XLA Ops:
  0.6 6.0 %collective-permute-start.2 = (bf16[16,32,128]{2,1,0:T(8,128)(2,1)}, bf16[16,32,128]{2,1,0:T(8,128)(2,1)S(1)}, u32[]{:S(2)}, u32[]{:S(2)}) collective-permute-start(bf16[16,32,128]{2,1,0:T(8,128)(2,1)} %param.9), channel_id=1, source_target_pairs={{4,0},{8,4},{12,8},{16,12},{20,16},{24,20},{28,24},{0,28},{5,1},{9... | collective-permute-start | bytes 393224 | tf_op jit(solution)/shard_map/ppermute | solution.py:19
  6.7 3.8 %collective-permute-start.3 = (bf16[16,32,128]{2,1,0:T(8,128)(2,1)}, bf16[16,32,128]{2,1,0:T(8,128)(2,1)S(1)}, u32[]{:S(2)}, u32[]{:S(2)}) collective-permute-start(bf16[16,32,128]{2,1,0:T(8,128)(2,1)} %param.9), channel_id=1, source_target_pairs={{8,0},{12,4},{16,8},{20,12},{24,16},{28,20},{0,24},{4,28},{9,1},{1... | collective-permute-start | bytes 393224 | tf_op jit(solution)/shard_map/ppermute | solution.py:19
  10.5 0.7 fusion.41
  11.2 0.7 broadcast_subtract_fusion
  12.5 0.7 convert_element_type.38
  13.3 5.2 %all_gather.15 = bf16[128,128]{1,0:T(8,128)(2,1)S(1)} all-gather(bf16[32,128]{1,0:T(8,128)(2,1)S(1)} %convert_element_type.38), channel_id=1, replica_groups=mesh['node'=8,'feat'=4] {'feat'}, dimensions={0}, use_global_device_ids=true | all-gather | bytes 40960 | tf_op jit(solution)/shard_map/all_gather | solution.py:77
  18.5 0.9 constant_dynamic-update-slice_fusion.2
  19.5 0.8 fusion.10
  20.3 7.2 %fusion.4 = f32[256,32,128]{2,1,0:T(8,128)S(1)} fusion(bf16[256,128,128]{2,1,0:T(8,128)(2,1)} %param.10, bf16[256,32,128]{2,0,1:T(8,128)(2,1)S(1)} %fusion.10), kind=kOutput, calls=%fused_computation.6 | convolution fusion | flops 268435456 | bytes 14680064 | tf_op jit(solution)/shard_map/tfk,tjk->tfj/dot_general | solution.py:69
  27.5 4.4 %fusion.7 = bf16[16,32,128]{2,0,1:T(8,128)(2,1)S(1)} fusion(f32[256,32,128]{2,1,0:T(8,128)S(1)} %fusion.4, f32[256]{0:T(256)S(1)} %compare_convert_fusion, s32[256]{0:T(256)S(1)} %broadcast_subtract_fusion), kind=kOutput, calls=%fused_computation.11 | convolution fusion | flops 201400320 | bytes 4327424 | tf_op jit(solution)/shard_map/tb,tfj->bfj/dot_general | solution.py:72
  31.9 7.3 %all_gather.16 = bf16[16,128,128]{2,0,1:T(8,128)(2,1)S(1)} all-gather(bf16[16,32,128]{2,0,1:T(8,128)(2,1)S(1)} %fusion.7), channel_id=1, replica_groups=mesh['node'=8,'feat'=4] {'feat'}, dimensions={1}, use_global_device_ids=true | all-gather | bytes 655360 | tf_op jit(solution)/shard_map/all_gather | solution.py:76
  39.1 1.1 fusion.16
  40.2 7.5 %all_gather.17 = bf16[16,128,128]{2,1,0:T(8,128)(2,1)S(1)} all-gather(bf16[16,32,128]{2,1,0:T(8,128)(2,1)S(1)} %get-tuple-element.22), channel_id=1, replica_groups=mesh['node'=8,'feat'=4] {'feat'}, dimensions={1}, use_global_device_ids=true | all-gather | bytes 655360 | tf_op jit(solution)/shard_map/all_gather | solution.py:86
  47.7 0.3 convolution_bitcast_fusion.1
  47.9 0.4 fusion.6
  48.5 0.7 fusion.34
  49.3 7.2 %fusion.5 = f32[256,32,128]{2,1,0:T(8,128)S(1)} fusion(bf16[256,128,128]{2,1,0:T(8,128)(2,1)} %param.10, bf16[256,32,128]{2,0,1:T(8,128)(2,1)S(1)} %fusion.34), kind=kOutput, calls=%fused_computation.7 | convolution fusion | flops 268435456 | bytes 14680064 | tf_op jit(solution)/shard_map/tfj,tjk->tfk/dot_general | solution.py:96
  56.5 4.9 %fusion = f32[80,32,128]{2,0,1:T(8,128)S(1)} fusion(f32[256,32,128]{2,1,0:T(8,128)S(1)} %fusion.5, f32[256]{0:T(256)S(1)} %compare_convert_fusion, s32[256]{0:T(256)S(1)} %fusion.41), kind=kOutput, calls=%fused_computation | convolution fusion | flops 1006673920 | bytes 5507072 | tf_op jit(solution)/shard_map/ts,tfk->sfk/dot_general | solution.py:99
  61.6 2.0 %collective-permute-start.7 = (f32[16,32,128]{2,0,1:T(8,128)S(1)}, f32[16,32,128]{2,0,1:T(8,128)S(1)}, u32[]{:S(2)}, u32[]{:S(2)}) collective-permute-start(f32[16,32,128]{2,0,1:T(8,128)S(1)} %get-tuple-element.19), channel_id=1, source_target_pairs={{24,0},{28,4},{0,8},{4,12},{8,16},{12,20},{16,24},{20,28},{25,1},{... | collective-permute-start | bytes 786440 | tf_op jit(solution)/shard_map/ppermute | solution.py:19
  63.6 1.5 %collective-permute-start.6 = (f32[16,32,128]{2,0,1:T(8,128)S(1)}, f32[16,32,128]{2,0,1:T(8,128)S(1)}, u32[]{:S(2)}, u32[]{:S(2)}) collective-permute-start(f32[16,32,128]{2,0,1:T(8,128)S(1)} %get-tuple-element.20), channel_id=1, source_target_pairs={{28,0},{0,4},{4,8},{8,12},{12,16},{16,20},{20,24},{24,28},{29,1},{... | collective-permute-start | bytes 786440 | tf_op jit(solution)/shard_map/ppermute | solution.py:19
  65.0 3.3 %collective-permute-start.5 = (f32[16,32,128]{2,0,1:T(8,128)S(1)}, f32[16,32,128]{2,0,1:T(8,128)S(1)}, u32[]{:S(2)}, u32[]{:S(2)}) collective-permute-start(f32[16,32,128]{2,0,1:T(8,128)S(1)} %get-tuple-element.21), channel_id=1, source_target_pairs={{4,0},{8,4},{12,8},{16,12},{20,16},{24,20},{28,24},{0,28},{5,1},{9... | collective-permute-start | bytes 786440 | tf_op jit(solution)/shard_map/ppermute | solution.py:19
  68.3 37.9 %all-gather = f32[256,128]{1,0:T(8,128)S(1)} all-gather(f32[32,128]{1,0:T(8,128)S(1)} %convolution_bitcast_fusion.1), channel_id=2, replica_groups=mesh['node'=8,'feat'=4] {'node'}, dimensions={0}, use_global_device_ids=true | all-gather | bytes 147456 | tf_op jit(solution)/shard_map/all_gather | solution.py:89
  106.2 1.4 %divide_subtract_fusion = (f32[32,128]{1,0:T(8,128)}, f32[32,128]{1,0:T(8,128)}, f32[32,128]{1,0:T(8,128)}) fusion(f32[32,128]{1,0:T(8,128)} %param.14, f32[32,128]{1,0:T(8,128)S(1)} %reduce_sum.9, f32[32,128]{1,0:T(8,128)} %param.15, f32[32,128]{1,0:T(8,128)} %param.16), kind=kLoop, calls=%fused_computation.39 | loop fusion | flops 53248 | bytes 114688 | tf_op jit(solution)/shard_map/sub | solution.py:107
  107.7 0.8 copy.21
  (22 shorter events, 0.6 us)
Async XLA Ops:
  0.6 18.8 %collective-permute-start.2 = (bf16[16,32,128]{2,1,0:T(8,128)(2,1)}, bf16[16,32,128]{2,1,0:T(8,128)(2,1)S(1)}, u32[]{:S(2)}, u32[]{:S(2)}) collective-permute-start(bf16[16,32,128]{2,1,0:T(8,128)(2,1)} %param.9), channel_id=1, source_target_pairs={{4,0},{8,4},{12,8},{16,12},{20,16},{24,20},{28,24},{0,28},{5,1},{9... | collective-permute-start | bytes 393224 | tf_op jit(solution)/shard_map/ppermute | solution.py:19
  6.7 11.8 %collective-permute-start.1 = (bf16[16,32,128]{2,1,0:T(8,128)(2,1)}, bf16[16,32,128]{2,1,0:T(8,128)(2,1)S(1)}, u32[]{:S(2)}, u32[]{:S(2)}) collective-permute-start(bf16[16,32,128]{2,1,0:T(8,128)(2,1)} %param.9), channel_id=1, source_target_pairs={{28,0},{0,4},{4,8},{8,12},{12,16},{16,20},{20,24},{24,28},{29,1},{... | collective-permute-start | bytes 393224 | tf_op jit(solution)/shard_map/ppermute | solution.py:19
  6.7 11.8 %collective-permute-start = (bf16[16,32,128]{2,1,0:T(8,128)(2,1)}, bf16[16,32,128]{2,1,0:T(8,128)(2,1)S(1)}, u32[]{:S(2)}, u32[]{:S(2)}) collective-permute-start(bf16[16,32,128]{2,1,0:T(8,128)(2,1)} %param.9), channel_id=1, source_target_pairs={{24,0},{28,4},{0,8},{4,12},{8,16},{12,20},{16,24},{20,28},{25,1},{... | collective-permute-start | bytes 393224 | tf_op jit(solution)/shard_map/ppermute | solution.py:19
  6.7 12.8 %collective-permute-start.3 = (bf16[16,32,128]{2,1,0:T(8,128)(2,1)}, bf16[16,32,128]{2,1,0:T(8,128)(2,1)S(1)}, u32[]{:S(2)}, u32[]{:S(2)}) collective-permute-start(bf16[16,32,128]{2,1,0:T(8,128)(2,1)} %param.9), channel_id=1, source_target_pairs={{8,0},{12,4},{16,8},{20,12},{24,16},{28,20},{0,24},{4,28},{9,1},{1... | collective-permute-start | bytes 393224 | tf_op jit(solution)/shard_map/ppermute | solution.py:19
  27.5 11.6 %copy-start = (bf16[16,32,128]{2,1,0:T(8,128)(2,1)S(1)}, bf16[16,32,128]{2,1,0:T(8,128)(2,1)}, u32[]{:S(2)}) copy-start(bf16[16,32,128]{2,1,0:T(8,128)(2,1)} %param.17) | copy-start | bytes 393220
  61.5 46.1 %collective-permute-start.4 = (f32[16,32,128]{2,0,1:T(8,128)S(1)}, f32[16,32,128]{2,0,1:T(8,128)S(1)}, u32[]{:S(2)}, u32[]{:S(2)}) collective-permute-start(f32[16,32,128]{2,0,1:T(8,128)S(1)} %get-tuple-element.18), channel_id=1, source_target_pairs={{8,0},{12,4},{16,8},{20,12},{24,16},{28,20},{0,24},{4,28},{9,1},{1... | collective-permute-start | bytes 786440 | tf_op jit(solution)/shard_map/ppermute | solution.py:19
  61.6 46.1 %collective-permute-start.7 = (f32[16,32,128]{2,0,1:T(8,128)S(1)}, f32[16,32,128]{2,0,1:T(8,128)S(1)}, u32[]{:S(2)}, u32[]{:S(2)}) collective-permute-start(f32[16,32,128]{2,0,1:T(8,128)S(1)} %get-tuple-element.19), channel_id=1, source_target_pairs={{24,0},{28,4},{0,8},{4,12},{8,16},{12,20},{16,24},{20,28},{25,1},{... | collective-permute-start | bytes 786440 | tf_op jit(solution)/shard_map/ppermute | solution.py:19
  63.6 44.1 %collective-permute-start.6 = (f32[16,32,128]{2,0,1:T(8,128)S(1)}, f32[16,32,128]{2,0,1:T(8,128)S(1)}, u32[]{:S(2)}, u32[]{:S(2)}) collective-permute-start(f32[16,32,128]{2,0,1:T(8,128)S(1)} %get-tuple-element.20), channel_id=1, source_target_pairs={{28,0},{0,4},{4,8},{8,12},{12,16},{16,20},{20,24},{24,28},{29,1},{... | collective-permute-start | bytes 786440 | tf_op jit(solution)/shard_map/ppermute | solution.py:19
  65.0 42.6 %collective-permute-start.5 = (f32[16,32,128]{2,0,1:T(8,128)S(1)}, f32[16,32,128]{2,0,1:T(8,128)S(1)}, u32[]{:S(2)}, u32[]{:S(2)}) collective-permute-start(f32[16,32,128]{2,0,1:T(8,128)S(1)} %get-tuple-element.21), channel_id=1, source_target_pairs={{4,0},{8,4},{12,8},{16,12},{20,16},{24,20},{28,24},{0,28},{5,1},{9... | collective-permute-start | bytes 786440 | tf_op jit(solution)/shard_map/ppermute | solution.py:19
